TPU v7x, 256 devices: a whole 4x4x8 slice. The times are simulated.
256 devices in a mesh: seq: 64 (over y, z, core), pb: 4 (over x).
Axes of the slice: x: 4, y: 4, z: 8, core: 2. Of those that a mesh axis runs over, the one named last changes fastest.
Arguments:
- tokens: bfloat16 [16384, 2048], P('seq'), may hold values from -0.119628906 to 0.119628906
- w_query: bfloat16 [2048, 2048], P(None, 'pb')
- w_key: bfloat16 [2048, 2048], P(None, 'pb')
- w_value: bfloat16 [2048, 2048], P(None, 'pb'), may hold values from -0.125 to 0.125
- w_out: bfloat16 [2048, 2048], P('pb'), may hold values from -0.125 to 0.125
- gain_attn: float32 [2048], replicated, may hold values from 0.1 to 1.9
- gain_embed: float32 [2048], replicated, may hold values from 0.1 to 1.9
- queries: bfloat16 [256, 32, 2048], P(('seq', 'pb')), may hold values from -0.125 to 0.125
- query_lengths: int32 [256], P(('seq', 'pb')), may hold values from 8 to 32
- group_lengths: int32 [128], replicated, may hold values from 1 to 1024, 16384 in all
- teacher: float32 [256, 128], P(('seq', 'pb')), may hold values from -12 to 12
Outputs:
- embedded: bfloat16 [16384, 2048], P('seq')
- scores: float32 [256, 128], P(('seq', 'pb'))
- score_gradient: float32 [256, 128], P(('seq', 'pb'))
- distill_loss: float32 [], replicated
Inputs may be any that keep to these rules, and one draw needn't show every extreme that they name: `group_lengths`: the groups cover the document in order: the lengths sum to 16384.
All inputs are finite; a program needn't handle non-finite values.
Results may differ from a plain program's by a relative error of at most 0.013.
Values may be sent and summed in bfloat16 or wider, within the bound.
No kernel may reach another device: no remote copies, remote signals or barrier semaphores. Data moves between devices by JAX's collectives and lax.ppermute only.
A program may use at most 128 MiB of HBM per device.

v0:
```python
import jax
import jax.numpy as jnp
from jax import lax
from jax.sharding import PartitionSpec as P

HD = 128
WIN = 2048
LQ = 32
EPSILON = 1e-06
SOFTMAX_TEMP = 0.1


def shifted_2(x, axis, by):
    count = lax.axis_size(axis)
    pairs = [(i, i + by) for i in range(count) if 0 <= i + by < count]
    return lax.ppermute(x, axis, pairs)


def rms_scale(values, gain):
    mean_sq = jnp.mean(values * values, axis=-1, keepdims=True)
    return values * lax.rsqrt(mean_sq + EPSILON) * gain


def segmented_max(values, group_id):
    span_len = values.shape[-1]
    stride = 1
    while stride < span_len:
        filler = jnp.full(values.shape[:-1] + (stride,), -jnp.inf, values.dtype)
        shifted = jnp.concatenate([filler, values[..., :-stride]], axis=-1)
        prior_id = jnp.concatenate([jnp.full((stride,), -1, jnp.int32), group_id[:-stride]])
        values = jnp.where((prior_id == group_id)[None, :], jnp.maximum(values, shifted), values)
        stride = stride * 2
    return values


def per_device(
    tokens,
    w_query,
    w_key,
    w_value,
    w_out,
    gain_attn,
    gain_embed,
    queries,
    query_lengths,
    group_lengths,
    teacher,
):
    shard_rows = tokens.shape[0]
    seq_count = lax.axis_size("seq")
    seq_place = lax.axis_index("seq")
    head_width = w_query.shape[1]
    heads_here = head_width // HD
    half_win = WIN // 2
    reach_count = half_win // shard_rows
    my_start = seq_place * shard_rows
    total_tokens = shard_rows * seq_count
    residual = tokens.astype(jnp.float32)
    normed = rms_scale(residual, gain_attn).astype(jnp.bfloat16)
    q_local = jnp.dot(normed, w_query, preferred_element_type=jnp.float32).astype(jnp.bfloat16)
    k_local = jnp.dot(normed, w_key, preferred_element_type=jnp.float32).astype(jnp.bfloat16)
    v_local = jnp.dot(normed, w_value, preferred_element_type=jnp.float32).astype(jnp.bfloat16)
    key_value = jnp.stack([k_local, v_local])
    earlier = [shifted_2(key_value, "seq", distance) for distance in range(reach_count, 0, -1)]
    later = [shifted_2(key_value, "seq", -distance) for distance in range(1, reach_count + 1)]
    window = jnp.concatenate(earlier + [key_value] + later, axis=1)
    span_rows = window.shape[1]
    q_pos = my_start + jnp.arange(shard_rows, dtype=jnp.int32)
    k_pos = my_start - reach_count * shard_rows + jnp.arange(span_rows, dtype=jnp.int32)
    in_window = (
        (jnp.abs(q_pos[:, None] - k_pos[None, :]) <= half_win)
        & (k_pos >= 0)[None, :]
        & (k_pos < total_tokens)[None, :]
    )
    q_heads = q_local.reshape(shard_rows, heads_here, HD)
    k_heads = window[0].reshape(span_rows, heads_here, HD)
    v_heads = window[1].reshape(span_rows, heads_here, HD)
    logits = jnp.einsum(
        "qhd,khd->hqk", q_heads, k_heads, preferred_element_type=jnp.float32
    ) * HD ** (-0.5)
    logits = jnp.where(in_window[None], logits, -jnp.inf)
    row_max = jnp.max(logits, axis=-1, keepdims=True)
    exp_terms = jnp.exp(logits - row_max)
    weights = (exp_terms / jnp.sum(exp_terms, axis=-1, keepdims=True)).astype(jnp.bfloat16)
    mixed = jnp.einsum("hqk,khd->qhd", weights, v_heads, preferred_element_type=jnp.float32)
    mixed = mixed.reshape(shard_rows, head_width).astype(jnp.bfloat16)
    partial_value = jnp.dot(mixed, w_out, preferred_element_type=jnp.float32)
    attn_sum = lax.psum(partial_value, "pb")
    embedded = rms_scale(residual + attn_sum, gain_embed).astype(jnp.bfloat16)
    group_end = jnp.cumsum(group_lengths)
    group_start = group_end - group_lengths
    group_id = jnp.sum((group_end[None, :] <= q_pos[:, None]).astype(jnp.int32), axis=1)
    last_local = jnp.clip(group_end - 1 - my_start, 0, shard_rows - 1)
    present = (group_start < my_start + shard_rows) & (group_end > my_start)
    q_piece = lax.all_gather(queries, "seq", axis=0, tiled=True)
    count = q_piece.shape[0]
    q_rows = q_piece.reshape(count * q_piece.shape[1], q_piece.shape[2])
    similar = jnp.einsum("td,rd->tr", q_rows, embedded, preferred_element_type=jnp.float32)
    running = segmented_max(similar, group_id)
    picked = jnp.take(running, last_local, axis=1)
    picked = jnp.where(present[None, :], picked, -jnp.inf)
    part_max = picked.reshape(count, q_piece.shape[1], picked.shape[-1])
    own_count = queries.shape[0]
    all_maxima = lax.pmax(part_max, "seq")
    token_max = lax.dynamic_slice_in_dim(all_maxima, seq_place * own_count, own_count, 0)
    live_mask = (jnp.arange(LQ, dtype=jnp.int32)[None, :] < query_lengths[:, None]).astype(
        jnp.float32
    )
    scores = (
        jnp.sum(token_max * live_mask[:, :, None], axis=1)
        / query_lengths.astype(jnp.float32)[:, None]
    )
    student_scores = scores / SOFTMAX_TEMP
    student_scores = student_scores - jnp.max(student_scores, axis=-1, keepdims=True)
    student_log_prob = student_scores - jnp.log(
        jnp.sum(jnp.exp(student_scores), axis=-1, keepdims=True)
    )
    target_scores = teacher / SOFTMAX_TEMP
    target_scores = target_scores - jnp.max(target_scores, axis=-1, keepdims=True)
    log_t = target_scores - jnp.log(jnp.sum(jnp.exp(target_scores), axis=-1, keepdims=True))
    teacher_prob = jnp.exp(log_t)
    kl_terms = jnp.sum(teacher_prob * (log_t - student_log_prob), axis=-1)
    query_count_all = own_count * seq_count * lax.axis_size("pb")
    distill_loss = lax.psum(jnp.sum(kl_terms), ("seq", "pb")) / query_count_all
    score_gradient = (jnp.exp(student_log_prob) - teacher_prob) / (SOFTMAX_TEMP * query_count_all)
    return (embedded, scores, score_gradient, distill_loss)


def solution(mesh):
    placed = (
        P("seq", None),
        P(None, "pb"),
        P(None, "pb"),
        P(None, "pb"),
        P("pb", None),
        P(),
        P(),
        P(("seq", "pb"), None, None),
        P(("seq", "pb")),
        P(),
        P(("seq", "pb"), None),
    )
    return jax.shard_map(
        per_device,
        mesh=mesh,
        in_specs=placed,
        out_specs=(P("seq", None), P(("seq", "pb"), None), P(("seq", "pb"), None), P()),
        check_vma=False,
    )
```

profile of v0, /device:TPU:1, one launch (start us, length us, event | category | flops | bytes accessed | tf_op | source)
XLA Modules:
  0.0 512.5 jit_solution(6274992664846566963)
XLA Ops:
  8.1 1.6 fusion.10
  9.8 2.8 fusion.15
  12.6 0.7 fusion.14
  13.4 0.7 copy-done.5
  14.1 0.8 pad_maximum_fusion
  14.9 6.5 %collective-permute-start = (bf16[2,256,512]{2,1,0:T(8,128)(2,1)}, bf16[2,256,512]{2,1,0:T(8,128)(2,1)}, u32[]{:S(2)}, u32[]{:S(2)}) collective-permute-start(bf16[2,256,512]{2,1,0:T(8,128)(2,1)} %pad_maximum_fusion), channel_id=1, source_target_pairs={{0,16},{4,20},{8,24},{12,28},{16,32},{20,36},{24,40},{28,44},{32,4... | collective-permute-start | bytes 1572872 | tf_op jit(solution)/shard_map/ppermute | solution.py:16
  21.5 7.0 %collective-permute-start.1 = (bf16[2,256,512]{2,1,0:T(8,128)(2,1)}, bf16[2,256,512]{2,1,0:T(8,128)(2,1)}, u32[]{:S(2)}, u32[]{:S(2)}) collective-permute-start(bf16[2,256,512]{2,1,0:T(8,128)(2,1)} %pad_maximum_fusion), channel_id=1, source_target_pairs={{0,12},{4,16},{8,20},{12,24},{16,28},{20,32},{24,36},{28,40},{32,4... | collective-permute-start | bytes 1572872 | tf_op jit(solution)/shard_map/ppermute | solution.py:16
  28.4 2.6 collective-permute-start.2
  31.1 1.9 collective-permute-start.3
  33.0 3.2 collective-permute-start.4
  36.3 1.7 fusion.9
  37.9 3.0 fusion.16
  41.0 1.4 collective-permute-start.5
  42.4 1.1 constant_dynamic-update-slice_fusion.8
  43.5 14.3 %collective-permute-done.1 = bf16[2,256,512]{2,1,0:T(8,128)(2,1)} collective-permute-done((bf16[2,256,512]{2,1,0:T(8,128)(2,1)}, bf16[2,256,512]{2,1,0:T(8,128)(2,1)}, u32[]{:S(2)}, u32[]{:S(2)}) %collective-permute-start.1) | collective-permute-done | bytes 524320 | tf_op jit(solution)/shard_map/ppermute | solution.py:16
  57.7 1.3 collective-permute-start.6
  59.0 1.1 constant_dynamic-update-slice_fusion.7
  60.1 10.9 %collective-permute-done.2 = bf16[2,256,512]{2,1,0:T(8,128)(2,1)} collective-permute-done((bf16[2,256,512]{2,1,0:T(8,128)(2,1)}, bf16[2,256,512]{2,1,0:T(8,128)(2,1)}, u32[]{:S(2)}, u32[]{:S(2)}) %collective-permute-start.2) | collective-permute-done | bytes 524320 | tf_op jit(solution)/shard_map/ppermute | solution.py:16
  71.0 1.3 collective-permute-start.7
  72.2 1.1 constant_dynamic-update-slice_fusion.6
  73.3 4.4 collective-permute-done.3
  77.7 1.1 constant_dynamic-update-slice_fusion.5
  78.9 1.1 constant_dynamic-update-slice_fusion.3
  80.0 17.2 %collective-permute-done.6 = bf16[2,256,512]{2,1,0:T(8,128)(2,1)S(1)} collective-permute-done((bf16[2,256,512]{2,1,0:T(8,128)(2,1)}, bf16[2,256,512]{2,1,0:T(8,128)(2,1)S(1)}, u32[]{:S(2)}, u32[]{:S(2)}) %collective-permute-start.6) | collective-permute-done | bytes 524320 | tf_op jit(solution)/shard_map/ppermute | solution.py:16
  97.2 8.1 %collective-permute-done.7 = bf16[2,256,512]{2,1,0:T(8,128)(2,1)S(1)} collective-permute-done((bf16[2,256,512]{2,1,0:T(8,128)(2,1)}, bf16[2,256,512]{2,1,0:T(8,128)(2,1)S(1)}, u32[]{:S(2)}, u32[]{:S(2)}) %collective-permute-start.7) | collective-permute-done | bytes 524320 | tf_op jit(solution)/shard_map/ppermute | solution.py:16
  105.4 2.4 fusion.39
  107.8 4.3 copy.34
  112.1 5.3 %reshape_squeeze.7 = bf16[2304,4,128]{2,1,0:T(4,128)(2,1)} reshape(bf16[1,2304,512]{2,1,0:T(8,128)(2,1)} %get-tuple-element.8) | data formatting | bytes 4718592 | tf_op jit(solution)/shard_map/reshape;squeeze | solution.py:76
  117.4 8.8 %fusion.40 = (f32[4,256]{1,0:T(4,128)S(1)}, f32[4,256,2304]{2,1,0:T(8,128)}) fusion(pred[256,2304]{1,0:T(8,128)(4,1)} %fusion.9, bf16[2304,4,128]{2,1,0:T(4,128)(2,1)} %reshape_squeeze.7, bf16[32,4,8,128]{3,2,1,0:T(8,128)(2,1)S(1)} %copy-done.13), kind=kOutput, calls=%fused_computation.89 | convolution fusion | flops 613419264 | bytes 12652544 | tf_op jit(solution)/shard_map/sub | solution.py:83
  126.2 6.2 %fusion.13 = bf16[4,128,256]{2,1,0:T(8,128)(2,1)S(1)} fusion(bf16[2304,4,128]{0,2,1:T(8,128)(2,1)} %bitcast.54, f32[4,256,2304]{2,1,0:T(8,128)} %get-tuple-element.23, f32[4,256]{1,0:T(4,128)S(1)} %get-tuple-element.22), kind=kOutput, calls=%fused_computation.32 | convolution fusion | flops 608829440 | bytes 12062720 | tf_op jit(solution)/shard_map/hqk,khd->qhd/dot_general | solution.py:85
  132.4 2.0 fusion.45
  134.5 0.5 all-gather.2.cloned.1.call-update
  135.0 0.2 all-reduce.20.cloned.1.call-start
  135.3 0.1 copy.32
  135.4 0.2 reduce-window.4
  135.7 0.2 convert_reduce_fusion
  136.0 66.0 %all-reduce.18.cloned.1.call-done = f32[256,2048]{1,0:T(8,128)} async-done(((f32[256,2048]{1,0:T(8,128)}), f32[256,2048]{1,0:T(8,128)}) %all-reduce.18.cloned.1.call-update) | async-done | bytes 2097168 | tf_op jit(solution)/shard_map/psum | solution.py:88
  202.0 2.1 multiply_reduce_fusion
  204.3 0.4 multiply_convert_fusion
  204.7 20.3 %all-gather.2.cloned.1.call-done = bf16[64,32,2048]{2,1,0:T(8,128)(2,1)} async-done(((bf16[1,32,2048]{2,1,0:T(8,128)(2,1)}), bf16[64,32,2048]{2,1,0:T(8,128)(2,1)}) %all-gather.2.cloned.1.call-update) | async-done | bytes 8388624 | tf_op jit(solution)/shard_map/all_gather | solution.py:95
  225.0 5.7 %convolution_bitcast_fusion = f32[2048,256]{0,1:T(8,128)S(1)} fusion(bf16[256,2048]{1,0:T(8,128)(2,1)S(1)} %multiply_convert_fusion, bf16[2048,2048]{1,0:T(8,128)(2,1)} %bitcast.65), kind=kOutput, calls=%fused_computation.21 | convolution fusion | flops 2147483648 | bytes 11534336 | tf_op jit(solution)/shard_map/td,rd->tr/dot_general | solution.py:98
  230.7 0.3 maximum_select_fusion.7
  231.1 0.4 maximum_select_fusion.6
  231.4 0.4 maximum_select_fusion.5
  231.8 0.2 slice.79
  232.0 0.3 maximum_select_fusion.4
  232.3 0.2 slice.80
  232.5 0.3 maximum_select_fusion.3
  232.8 0.2 slice.81
  233.0 0.3 maximum_select_fusion.2
  233.4 0.1 slice.82
  233.5 0.3 maximum_select_fusion.1
  233.9 0.3 maximum_select_fusion
  234.2 1.0 gather_fusion
  235.2 1.4 copy.33
  236.6 2.4 select_select_fusion
  239.6 0.6 multiply_reduce_fusion.3
  240.3 1.2 exponential_reduce_fusion
  242.2 178.2 %all-reduce.20.cloned.1.call-done = f32[64,32,128]{2,1,0:T(8,128)} async-done(((f32[64,32,128]{2,1,0:T(8,128)}), f32[64,32,128]{2,1,0:T(8,128)}) %all-reduce.20.cloned.1.call-update) | async-done | bytes 1048592 | tf_op jit(solution)/shard_map/pmax | solution.py:104
  420.3 0.8 multiply_reduce_fusion.1
  421.2 0.6 multiply_reduce_fusion.4
  421.8 1.3 exponential_reduce_fusion.1
  423.7 2.5 multiply_reduce_fusion.2
  426.2 77.1 %psum.15 = f32[]{:T(128)} all-reduce(f32[]{:T(128)} %get-tuple-element.10), channel_id=1, replica_groups=mesh['seq'=64,'pb'=4] {'seq','pb'}, use_global_device_ids=true, to_apply=%region_14.15 | all-reduce | flops 1 | bytes 8 | tf_op jit(solution)/shard_map/psum | solution.py:124
  (50 shorter events, 0.8 us)
Async XLA Ops:
  8.0 124.4 %copy-start = (bf16[512,2048]{1,0:T(8,128)(2,1)S(1)}, bf16[512,2048]{1,0:T(8,128)(2,1)}, u32[]{:S(2)}) copy-start(bf16[512,2048]{1,0:T(8,128)(2,1)} %param.15) | copy-start | bytes 6291460
  8.0 194.0 %all-reduce.18.cloned.1.call-start = ((), (), s32[]{:S(2)}) async-start(), calls=%async_computation | async-start | bytes 4194304 | tf_op jit(solution)/shard_map/psum | solution.py:88
  9.7 2.9 copy-start.2
  9.7 2.9 copy-start.11
  9.7 2.9 copy-start.12
  13.4 0.7 copy-start.5
  14.9 26.0 %collective-permute-start = (bf16[2,256,512]{2,1,0:T(8,128)(2,1)}, bf16[2,256,512]{2,1,0:T(8,128)(2,1)}, u32[]{:S(2)}, u32[]{:S(2)}) collective-permute-start(bf16[2,256,512]{2,1,0:T(8,128)(2,1)} %pad_maximum_fusion), channel_id=1, source_target_pairs={{0,16},{4,20},{8,24},{12,28},{16,32},{20,36},{24,40},{28,44},{32,4... | collective-permute-start | bytes 1572872 | tf_op jit(solution)/shard_map/ppermute | solution.py:16
  21.5 36.2 %collective-permute-start.1 = (bf16[2,256,512]{2,1,0:T(8,128)(2,1)}, bf16[2,256,512]{2,1,0:T(8,128)(2,1)}, u32[]{:S(2)}, u32[]{:S(2)}) collective-permute-start(bf16[2,256,512]{2,1,0:T(8,128)(2,1)} %pad_maximum_fusion), channel_id=1, source_target_pairs={{0,12},{4,16},{8,20},{12,24},{16,28},{20,32},{24,36},{28,40},{32,4... | collective-permute-start | bytes 1572872 | tf_op jit(solution)/shard_map/ppermute | solution.py:16
  28.4 42.5 %collective-permute-start.2 = (bf16[2,256,512]{2,1,0:T(8,128)(2,1)}, bf16[2,256,512]{2,1,0:T(8,128)(2,1)}, u32[]{:S(2)}, u32[]{:S(2)}) collective-permute-start(bf16[2,256,512]{2,1,0:T(8,128)(2,1)} %pad_maximum_fusion), channel_id=1, source_target_pairs={{0,8},{4,12},{8,16},{12,20},{16,24},{20,28},{24,32},{28,36},{32,40... | collective-permute-start | bytes 1572872 | tf_op jit(solution)/shard_map/ppermute | solution.py:16
  31.1 46.6 %collective-permute-start.3 = (bf16[2,256,512]{2,1,0:T(8,128)(2,1)}, bf16[2,256,512]{2,1,0:T(8,128)(2,1)}, u32[]{:S(2)}, u32[]{:S(2)}) collective-permute-start(bf16[2,256,512]{2,1,0:T(8,128)(2,1)} %pad_maximum_fusion), channel_id=1, source_target_pairs={{0,4},{4,8},{8,12},{12,16},{16,20},{20,24},{24,28},{28,32},{32,36}... | collective-permute-start | bytes 1572872 | tf_op jit(solution)/shard_map/ppermute | solution.py:16
  33.0 45.9 %collective-permute-start.4 = (bf16[2,256,512]{2,1,0:T(8,128)(2,1)}, bf16[2,256,512]{2,1,0:T(8,128)(2,1)}, u32[]{:S(2)}, u32[]{:S(2)}) collective-permute-start(bf16[2,256,512]{2,1,0:T(8,128)(2,1)} %pad_maximum_fusion), channel_id=1, source_target_pairs={{4,0},{8,4},{12,8},{16,12},{20,16},{24,20},{28,24},{32,28},{36,32}... | collective-permute-start | bytes 1572872 | tf_op jit(solution)/shard_map/ppermute | solution.py:16
  41.0 37.8 %copy-start.6 = (bf16[1,256,512]{2,1,0:T(8,128)(2,1)S(1)}, bf16[1,256,512]{2,1,0:T(8,128)(2,1)}, u32[]{:S(2)}) copy-start(bf16[1,256,512]{2,1,0:T(8,128)(2,1)} %copy-done.5) | copy-start | bytes 786436
  41.0 39.0 %collective-permute-start.5 = (bf16[2,256,512]{2,1,0:T(8,128)(2,1)}, bf16[2,256,512]{2,1,0:T(8,128)(2,1)S(1)}, u32[]{:S(2)}, u32[]{:S(2)}) collective-permute-start(bf16[2,256,512]{2,1,0:T(8,128)(2,1)} %pad_maximum_fusion), channel_id=1, source_target_pairs={{8,0},{12,4},{16,8},{20,12},{24,16},{28,20},{32,24},{36,28},{40,32... | collective-permute-start | bytes 1572872 | tf_op jit(solution)/shard_map/ppermute | solution.py:16
  57.7 39.4 %collective-permute-start.6 = (bf16[2,256,512]{2,1,0:T(8,128)(2,1)}, bf16[2,256,512]{2,1,0:T(8,128)(2,1)S(1)}, u32[]{:S(2)}, u32[]{:S(2)}) collective-permute-start(bf16[2,256,512]{2,1,0:T(8,128)(2,1)} %pad_maximum_fusion), channel_id=1, source_target_pairs={{12,0},{16,4},{20,8},{24,12},{28,16},{32,20},{36,24},{40,28},{44,3... | collective-permute-start | bytes 1572872 | tf_op jit(solution)/shard_map/ppermute | solution.py:16
  71.0 34.4 %collective-permute-start.7 = (bf16[2,256,512]{2,1,0:T(8,128)(2,1)}, bf16[2,256,512]{2,1,0:T(8,128)(2,1)S(1)}, u32[]{:S(2)}, u32[]{:S(2)}) collective-permute-start(bf16[2,256,512]{2,1,0:T(8,128)(2,1)} %pad_maximum_fusion), channel_id=1, source_target_pairs={{16,0},{20,4},{24,8},{28,12},{32,16},{36,20},{40,24},{44,28},{48,3... | collective-permute-start | bytes 1572872 | tf_op jit(solution)/shard_map/ppermute | solution.py:16
  112.1 5.3 %copy-start.13 = (bf16[32,4,8,128]{3,2,1,0:T(8,128)(2,1)S(1)}, bf16[32,4,8,128]{3,2,1,0:T(8,128)(2,1)}, u32[]{:S(2)}) copy-start(bf16[32,4,8,128]{3,2,1,0:T(8,128)(2,1)} %fusion.16) | copy-start | bytes 786436
  134.4 0.8 copy-start.8
  134.4 69.7 %copy-start.7 = (f32[2048]{0:T(1024)S(1)}, f32[2048]{0:T(1024)}, u32[]{:S(2)}) copy-start(f32[2048]{0:T(1024)} %param.17) | copy-start | bytes 24580
  134.5 90.5 %all-gather.2.cloned.1.call-start = ((), (), s32[]{:S(2)}) async-start(), calls=%async_computation.1 | async-start | bytes 8519680 | tf_op jit(solution)/shard_map/all_gather | solution.py:95
  135.0 285.3 %all-reduce.20.cloned.1.call-start = ((), (), s32[]{:S(2)}) async-start(), calls=%async_computation.2 | async-start | bytes 2097152 | tf_op jit(solution)/shard_map/pmax | solution.py:104
  202.0 2.3 copy-start.3
  204.6 26.1 %copy-start.4 = (bf16[256,2048]{1,0:T(8,128)(2,1)}, bf16[256,2048]{1,0:T(8,128)(2,1)S(1)}, u32[]{:S(2)}) copy-start(bf16[256,2048]{1,0:T(8,128)(2,1)S(1)} %multiply_convert_fusion) | copy-start | bytes 3145732
  235.2 268.7 %copy-start.1 = (bf16[512,2048]{1,0:T(8,128)(2,1)S(1)}, bf16[512,2048]{1,0:T(8,128)(2,1)}, u32[]{:S(2)}) copy-start(bf16[512,2048]{1,0:T(8,128)(2,1)} %param.15) | copy-start | bytes 6291460
  236.6 3.0 copy-start.10
  421.8 82.2 %copy-start.9 = (f32[128]{0:T(128)}, f32[128]{0:T(128)S(1)}, u32[]{:S(2)}) copy-start(f32[128]{0:T(128)S(1)} %get-tuple-element.7) | copy-start | bytes 1540
Sparse Core Ops, SparseCore 0:
  134.6 67.3 all-reduce.17
Sparse Core Ops, SparseCore 1:
  137.7 87.2 all-gather.1
  239.1 181.2 all-reduce.19
where the time goes:
time: 514 us; the launch traced here: 513 us
  waiting for transfers between devices  320 us (62%)
  blocking collectives  77.1 us (15%)
  matrix products  29.3 us (6%)
  starting transfers between devices  25.5 us (5%)
  local copies, waits for them, and re-layouts  21.7 us (4%)
  between operations  19.7 us (4%)
  other arithmetic  19.2 us (4%)
    pmax x1, waiting for transfers between devices, per_device(): all_maxima = lax.pmax(part_max, 'seq')  178 us
    psum x1, blocking collectives, per_device(): distill_loss = lax.psum(jnp.sum(kl_terms), ('seq', 'pb')) / query_count_all  77.1 us
    psum x1, waiting for transfers between devices, per_device(): attn_sum = lax.psum(partial_value, 'pb')  66 us
    ppermute x8, waiting for transfers between devices, shifted_2(): return lax.ppermute(x, axis, pairs)  54.8 us
    ppermute x8, starting transfers between devices, shifted_2(): return lax.ppermute(x, axis, pairs)  25.2 us
    all_gather x1, waiting for transfers between devices, per_device(): q_piece = lax.all_gather(queries, 'seq', axis=0, tiled=True)  20.3 us
  transfers between devices with their start and end apart: 11, of which 8 were waited for; matrix products, arithmetic and copies ran while one was open for 3% of the time, Pallas kernels for 0%

commit v1 on v0

--- a/solution.py
+++ b/solution.py
@@ -85,7 +85,9 @@
     mixed = jnp.einsum("hqk,khd->qhd", weights, v_heads, preferred_element_type=jnp.float32)
     mixed = mixed.reshape(shard_rows, head_width).astype(jnp.bfloat16)
     partial_value = jnp.dot(mixed, w_out, preferred_element_type=jnp.float32)
-    attn_sum = lax.psum(partial_value, "pb")
+    attn_sum = partial_value
+    for hop in (1, 2):
+        attn_sum = attn_sum + lax.ppermute(attn_sum, "pb", [(dev, dev ^ hop) for dev in range(4)])
     embedded = rms_scale(residual + attn_sum, gain_embed).astype(jnp.bfloat16)
     group_end = jnp.cumsum(group_lengths)
     group_start = group_end - group_lengths

time: 514 us -> 555 us (1.080)
  waiting for transfers between devices: 320 us -> 357 us
    ppermute x0 -> x2, waiting for transfers between devices: none -> 86.8 us  [per_device(): lax.ppermute(attn_sum, 'pb', [(dev, dev ^ hop) for dev in range(4)])]
    psum x1 -> x0, waiting for transfers between devices: 66 us -> none  [per_device(): attn_sum = lax.psum(partial_value, 'pb')]
    ppermute x8, waiting for transfers between devices: 54.8 us -> 78.1 us  [shifted_2(): return lax.ppermute(x, axis, pairs)]
    all_gather x1, waiting for transfers between devices: 20.3 us -> 0.01 us  [per_device(): q_piece = lax.all_gather(queries, 'seq', axis=0, tiled=True)]
    pmax x1, waiting for transfers between devices: 178 us -> 191 us  [per_device(): all_maxima = lax.pmax(part_max, 'seq')]
  transfers between devices with their start and end apart: 11 -> 12, of which waited for: 8 -> 8; matrix products, arithmetic and copies ran while one was open for 3% -> 9% of each run, Pallas kernels for 0% -> 0%
where the time goes in v1:
time: 555 us; the launch traced here: 554 us
  waiting for transfers between devices  357 us (64%)
  blocking collectives  77.2 us (14%)
  starting transfers between devices  29.4 us (5%)
  matrix products  28.4 us (5%)
  other arithmetic  22 us (4%)
  local copies, waits for them, and re-layouts  21.7 us (4%)
  between operations  18.3 us (3%)
    pmax x1, waiting for transfers between devices, per_device(): all_maxima = lax.pmax(part_max, 'seq')  191 us
    ppermute x2, waiting for transfers between devices, per_device(): lax.ppermute(attn_sum, 'pb', [(dev, dev ^ hop) for dev in range(4)])  86.8 us
    ppermute x8, waiting for transfers between devices, shifted_2(): return lax.ppermute(x, axis, pairs)  78.1 us
    psum x1, blocking collectives, per_device(): distill_loss = lax.psum(jnp.sum(kl_terms), ('seq', 'pb')) / query_count_all  77.2 us
    ppermute x8, starting transfers between devices, shifted_2(): return lax.ppermute(x, axis, pairs)  25.2 us
  transfers between devices with their start and end apart: 12, of which 8 were waited for; matrix products, arithmetic and copies ran while one was open for 9% of the time, Pallas kernels for 0%

profile of v1, /device:TPU:1, one launch (start us, length us, event | category | flops | bytes accessed | tf_op | source)
XLA Modules:
  0.0 553.5 jit_solution(8464645964514912757)
XLA Ops:
  7.2 0.7 all-gather.2.cloned.1.call-update
  8.0 1.5 fusion.10
  9.5 2.8 fusion.15
  12.4 0.7 fusion.14
  13.2 0.7 copy-done.3
  13.9 0.8 pad_maximum_fusion
  14.7 6.5 %collective-permute-start = (bf16[2,256,512]{2,1,0:T(8,128)(2,1)}, bf16[2,256,512]{2,1,0:T(8,128)(2,1)}, u32[]{:S(2)}, u32[]{:S(2)}) collective-permute-start(bf16[2,256,512]{2,1,0:T(8,128)(2,1)} %pad_maximum_fusion), channel_id=1, source_target_pairs={{0,16},{4,20},{8,24},{12,28},{16,32},{20,36},{24,40},{28,44},{32,4... | collective-permute-start | bytes 1572872 | tf_op jit(solution)/shard_map/ppermute | solution.py:16
  21.2 7.0 %collective-permute-start.1 = (bf16[2,256,512]{2,1,0:T(8,128)(2,1)}, bf16[2,256,512]{2,1,0:T(8,128)(2,1)}, u32[]{:S(2)}, u32[]{:S(2)}) collective-permute-start(bf16[2,256,512]{2,1,0:T(8,128)(2,1)} %pad_maximum_fusion), channel_id=1, source_target_pairs={{0,12},{4,16},{8,20},{12,24},{16,28},{20,32},{24,36},{28,40},{32,4... | collective-permute-start | bytes 1572872 | tf_op jit(solution)/shard_map/ppermute | solution.py:16
  28.2 2.6 collective-permute-start.2
  30.8 1.9 collective-permute-start.3
  32.7 3.2 collective-permute-start.4
  36.0 1.7 fusion.9
  37.7 3.1 fusion.16
  40.7 1.4 collective-permute-start.5
  42.1 1.1 constant_dynamic-update-slice_fusion.8
  43.2 19.2 %collective-permute-done.1 = bf16[2,256,512]{2,1,0:T(8,128)(2,1)} collective-permute-done((bf16[2,256,512]{2,1,0:T(8,128)(2,1)}, bf16[2,256,512]{2,1,0:T(8,128)(2,1)}, u32[]{:S(2)}, u32[]{:S(2)}) %collective-permute-start.1) | collective-permute-done | bytes 524320 | tf_op jit(solution)/shard_map/ppermute | solution.py:16
  62.4 1.3 collective-permute-start.6
  63.7 1.1 constant_dynamic-update-slice_fusion.7
  64.8 13.6 %collective-permute-done.2 = bf16[2,256,512]{2,1,0:T(8,128)(2,1)} collective-permute-done((bf16[2,256,512]{2,1,0:T(8,128)(2,1)}, bf16[2,256,512]{2,1,0:T(8,128)(2,1)}, u32[]{:S(2)}, u32[]{:S(2)}) %collective-permute-start.2) | collective-permute-done | bytes 524320 | tf_op jit(solution)/shard_map/ppermute | solution.py:16
  78.3 1.3 collective-permute-start.7
  79.6 1.1 constant_dynamic-update-slice_fusion.6
  80.7 10.8 %collective-permute-done.3 = bf16[2,256,512]{2,1,0:T(8,128)(2,1)} collective-permute-done((bf16[2,256,512]{2,1,0:T(8,128)(2,1)}, bf16[2,256,512]{2,1,0:T(8,128)(2,1)}, u32[]{:S(2)}, u32[]{:S(2)}) %collective-permute-start.3) | collective-permute-done | bytes 524320 | tf_op jit(solution)/shard_map/ppermute | solution.py:16
  91.5 1.1 constant_dynamic-update-slice_fusion.5
  92.7 1.1 constant_dynamic-update-slice_fusion.3
  93.8 9.0 %collective-permute-done.6 = bf16[2,256,512]{2,1,0:T(8,128)(2,1)S(1)} collective-permute-done((bf16[2,256,512]{2,1,0:T(8,128)(2,1)}, bf16[2,256,512]{2,1,0:T(8,128)(2,1)S(1)}, u32[]{:S(2)}, u32[]{:S(2)}) %collective-permute-start.6) | collective-permute-done | bytes 524320 | tf_op jit(solution)/shard_map/ppermute | solution.py:16
  102.8 25.6 %collective-permute-done.7 = bf16[2,256,512]{2,1,0:T(8,128)(2,1)S(1)} collective-permute-done((bf16[2,256,512]{2,1,0:T(8,128)(2,1)}, bf16[2,256,512]{2,1,0:T(8,128)(2,1)S(1)}, u32[]{:S(2)}, u32[]{:S(2)}) %collective-permute-start.7) | collective-permute-done | bytes 524320 | tf_op jit(solution)/shard_map/ppermute | solution.py:16
  128.4 2.4 fusion.39
  130.9 4.4 copy.34
  135.2 5.3 reshape_squeeze.7
  140.6 8.8 %fusion.40 = (f32[4,256]{1,0:T(4,128)S(1)}, f32[4,256,2304]{2,1,0:T(8,128)}) fusion(pred[256,2304]{1,0:T(8,128)(4,1)} %fusion.9, bf16[2304,4,128]{2,1,0:T(4,128)(2,1)} %reshape_squeeze.7, bf16[32,4,8,128]{3,2,1,0:T(8,128)(2,1)S(1)} %copy-done.11), kind=kOutput, calls=%fused_computation.89 | convolution fusion | flops 613419264 | bytes 12652544 | tf_op jit(solution)/shard_map/sub | solution.py:83
  149.4 6.1 %fusion.13 = bf16[4,128,256]{2,1,0:T(8,128)(2,1)S(1)} fusion(bf16[2304,4,128]{0,2,1:T(8,128)(2,1)} %bitcast.54, f32[4,256,2304]{2,1,0:T(8,128)} %get-tuple-element.23, f32[4,256]{1,0:T(4,128)S(1)} %get-tuple-element.22), kind=kOutput, calls=%fused_computation.32 | convolution fusion | flops 608829440 | bytes 12062720 | tf_op jit(solution)/shard_map/hqk,khd->qhd/dot_general | solution.py:85
  155.5 0.7 fusion.45
  156.3 1.2 collective-permute-start.8
  157.5 42.7 %collective-permute-done.8 = f32[256,2048]{1,0:T(8,128)S(1)} collective-permute-done((f32[256,2048]{1,0:T(8,128)S(1)}, f32[256,2048]{1,0:T(8,128)S(1)}, u32[]{:S(2)}, u32[]{:S(2)}) %collective-permute-start.8) | collective-permute-done | bytes 2097184 | tf_op jit(solution)/shard_map/ppermute | solution.py:90
  200.2 0.3 add.126
  200.5 2.9 collective-permute-start.9
  203.5 0.2 reduce-window.4
  203.8 0.2 convert_reduce_fusion
  204.1 44.1 %collective-permute-done.9 = f32[256,2048]{1,0:T(8,128)} collective-permute-done((f32[256,2048]{1,0:T(8,128)S(1)}, f32[256,2048]{1,0:T(8,128)}, u32[]{:S(2)}, u32[]{:S(2)}) %collective-permute-start.9) | collective-permute-done | bytes 2097184 | tf_op jit(solution)/shard_map/ppermute | solution.py:90
  248.2 2.0 multiply_reduce_fusion
  250.2 3.1 multiply_convert_fusion
  253.3 6.1 %convolution_bitcast_fusion = f32[2048,256]{0,1:T(8,128)S(1)} fusion(bf16[256,2048]{1,0:T(8,128)(2,1)} %multiply_convert_fusion, bf16[2048,2048]{1,0:T(8,128)(2,1)} %bitcast.65), kind=kOutput, calls=%fused_computation.21 | convolution fusion | flops 2147483648 | bytes 11534336 | tf_op jit(solution)/shard_map/td,rd->tr/dot_general | solution.py:100
  259.4 0.3 maximum_select_fusion.7
  259.8 0.4 maximum_select_fusion.6
  260.1 0.4 maximum_select_fusion.5
  260.5 0.2 slice.79
  260.7 0.3 maximum_select_fusion.4
  261.0 0.2 slice.80
  261.2 0.3 maximum_select_fusion.3
  261.5 0.2 slice.81
  261.7 0.3 maximum_select_fusion.2
  262.2 0.3 maximum_select_fusion.1
  262.6 0.3 maximum_select_fusion
  262.9 1.0 gather_fusion
  263.9 1.4 copy.33
  265.3 2.4 select_select_fusion
  268.3 0.6 multiply_reduce_fusion.3
  268.9 1.2 exponential_reduce_fusion
  270.9 191.0 %all-reduce.17.cloned.1.call-done = f32[64,32,128]{2,1,0:T(8,128)} async-done(((f32[64,32,128]{2,1,0:T(8,128)}), f32[64,32,128]{2,1,0:T(8,128)}) %all-reduce.17.cloned.1.call-update) | async-done | bytes 1048592 | tf_op jit(solution)/shard_map/pmax | solution.py:106
  461.9 0.8 multiply_reduce_fusion.1
  462.7 0.6 multiply_reduce_fusion.4
  463.3 1.3 exponential_reduce_fusion.1
  465.2 2.5 multiply_reduce_fusion.2
  467.7 77.2 %psum.7 = f32[]{:T(128)} all-reduce(f32[]{:T(128)} %get-tuple-element.10), channel_id=1, replica_groups=mesh['seq'=64,'pb'=4] {'seq','pb'}, use_global_device_ids=true, to_apply=%region_13.14 | all-reduce | flops 1 | bytes 8 | tf_op jit(solution)/shard_map/psum | solution.py:126
  (48 shorter events, 0.9 us)
Async XLA Ops:
  7.2 148.4 %copy-start = (bf16[512,2048]{1,0:T(8,128)(2,1)S(1)}, bf16[512,2048]{1,0:T(8,128)(2,1)}, u32[]{:S(2)}) copy-start(bf16[512,2048]{1,0:T(8,128)(2,1)} %param.15) | copy-start | bytes 6291460
  7.2 246.1 %all-gather.2.cloned.1.call-start = ((), (), s32[]{:S(2)}) async-start(), calls=%async_computation | async-start | bytes 8519680 | tf_op jit(solution)/shard_map/all_gather | solution.py:97
  7.9 454.0 %all-reduce.17.cloned.1.call-start = ((), (), s32[]{:S(2)}) async-start(), calls=%async_computation.1 | async-start | bytes 2097152 | tf_op jit(solution)/shard_map/pmax | solution.py:106
  9.5 2.9 copy-start.2
  9.5 2.9 copy-start.9
  9.5 2.9 copy-start.10
  13.1 0.7 copy-start.3
  14.7 26.0 %collective-permute-start = (bf16[2,256,512]{2,1,0:T(8,128)(2,1)}, bf16[2,256,512]{2,1,0:T(8,128)(2,1)}, u32[]{:S(2)}, u32[]{:S(2)}) collective-permute-start(bf16[2,256,512]{2,1,0:T(8,128)(2,1)} %pad_maximum_fusion), channel_id=1, source_target_pairs={{0,16},{4,20},{8,24},{12,28},{16,32},{20,36},{24,40},{28,44},{32,4... | collective-permute-start | bytes 1572872 | tf_op jit(solution)/shard_map/ppermute | solution.py:16
  21.2 41.2 %collective-permute-start.1 = (bf16[2,256,512]{2,1,0:T(8,128)(2,1)}, bf16[2,256,512]{2,1,0:T(8,128)(2,1)}, u32[]{:S(2)}, u32[]{:S(2)}) collective-permute-start(bf16[2,256,512]{2,1,0:T(8,128)(2,1)} %pad_maximum_fusion), channel_id=1, source_target_pairs={{0,12},{4,16},{8,20},{12,24},{16,28},{20,32},{24,36},{28,40},{32,4... | collective-permute-start | bytes 1572872 | tf_op jit(solution)/shard_map/ppermute | solution.py:16
  28.2 50.2 %collective-permute-start.2 = (bf16[2,256,512]{2,1,0:T(8,128)(2,1)}, bf16[2,256,512]{2,1,0:T(8,128)(2,1)}, u32[]{:S(2)}, u32[]{:S(2)}) collective-permute-start(bf16[2,256,512]{2,1,0:T(8,128)(2,1)} %pad_maximum_fusion), channel_id=1, source_target_pairs={{0,8},{4,12},{8,16},{12,20},{16,24},{20,28},{24,32},{28,36},{32,40... | collective-permute-start | bytes 1572872 | tf_op jit(solution)/shard_map/ppermute | solution.py:16
  30.8 60.7 %collective-permute-start.3 = (bf16[2,256,512]{2,1,0:T(8,128)(2,1)}, bf16[2,256,512]{2,1,0:T(8,128)(2,1)}, u32[]{:S(2)}, u32[]{:S(2)}) collective-permute-start(bf16[2,256,512]{2,1,0:T(8,128)(2,1)} %pad_maximum_fusion), channel_id=1, source_target_pairs={{0,4},{4,8},{8,12},{12,16},{16,20},{20,24},{24,28},{28,32},{32,36}... | collective-permute-start | bytes 1572872 | tf_op jit(solution)/shard_map/ppermute | solution.py:16
  32.7 60.0 %collective-permute-start.4 = (bf16[2,256,512]{2,1,0:T(8,128)(2,1)}, bf16[2,256,512]{2,1,0:T(8,128)(2,1)}, u32[]{:S(2)}, u32[]{:S(2)}) collective-permute-start(bf16[2,256,512]{2,1,0:T(8,128)(2,1)} %pad_maximum_fusion), channel_id=1, source_target_pairs={{4,0},{8,4},{12,8},{16,12},{20,16},{24,20},{28,24},{32,28},{36,32}... | collective-permute-start | bytes 1572872 | tf_op jit(solution)/shard_map/ppermute | solution.py:16
  40.7 51.9 %copy-start.4 = (bf16[1,256,512]{2,1,0:T(8,128)(2,1)S(1)}, bf16[1,256,512]{2,1,0:T(8,128)(2,1)}, u32[]{:S(2)}) copy-start(bf16[1,256,512]{2,1,0:T(8,128)(2,1)} %copy-done.3) | copy-start | bytes 786436
  40.7 53.1 %collective-permute-start.5 = (bf16[2,256,512]{2,1,0:T(8,128)(2,1)}, bf16[2,256,512]{2,1,0:T(8,128)(2,1)S(1)}, u32[]{:S(2)}, u32[]{:S(2)}) collective-permute-start(bf16[2,256,512]{2,1,0:T(8,128)(2,1)} %pad_maximum_fusion), channel_id=1, source_target_pairs={{8,0},{12,4},{16,8},{20,12},{24,16},{28,20},{32,24},{36,28},{40,32... | collective-permute-start | bytes 1572872 | tf_op jit(solution)/shard_map/ppermute | solution.py:16
  62.4 40.4 %collective-permute-start.6 = (bf16[2,256,512]{2,1,0:T(8,128)(2,1)}, bf16[2,256,512]{2,1,0:T(8,128)(2,1)S(1)}, u32[]{:S(2)}, u32[]{:S(2)}) collective-permute-start(bf16[2,256,512]{2,1,0:T(8,128)(2,1)} %pad_maximum_fusion), channel_id=1, source_target_pairs={{12,0},{16,4},{20,8},{24,12},{28,16},{32,20},{36,24},{40,28},{44,3... | collective-permute-start | bytes 1572872 | tf_op jit(solution)/shard_map/ppermute | solution.py:16
  78.3 50.1 %collective-permute-start.7 = (bf16[2,256,512]{2,1,0:T(8,128)(2,1)}, bf16[2,256,512]{2,1,0:T(8,128)(2,1)S(1)}, u32[]{:S(2)}, u32[]{:S(2)}) collective-permute-start(bf16[2,256,512]{2,1,0:T(8,128)(2,1)} %pad_maximum_fusion), channel_id=1, source_target_pairs={{16,0},{20,4},{24,8},{28,12},{32,16},{36,20},{40,24},{44,28},{48,3... | collective-permute-start | bytes 1572872 | tf_op jit(solution)/shard_map/ppermute | solution.py:16
  135.2 5.3 copy-start.11
  156.3 47.1 %copy-start.6 = (s32[128]{0:T(128)S(1)}, s32[128]{0:T(128)}, u32[]{:S(2)}) copy-start(s32[128]{0:T(128)} %param.20) | copy-start | bytes 1540
  156.3 43.9 %collective-permute-start.8 = (f32[256,2048]{1,0:T(8,128)S(1)}, f32[256,2048]{1,0:T(8,128)S(1)}, u32[]{:S(2)}, u32[]{:S(2)}) collective-permute-start(f32[256,2048]{1,0:T(8,128)S(1)} %fusion.45), channel_id=1, source_target_pairs={{0,1},{1,0},{2,3},{3,2},{4,5},{5,4},{6,7},{7,6},{8,9},{9,8},{10,11... | collective-permute-start | bytes 6291464 | tf_op jit(solution)/shard_map/ppermute | solution.py:90
  200.5 47.7 %collective-permute-start.9 = (f32[256,2048]{1,0:T(8,128)S(1)}, f32[256,2048]{1,0:T(8,128)}, u32[]{:S(2)}, u32[]{:S(2)}) collective-permute-start(f32[256,2048]{1,0:T(8,128)S(1)} %add.126), channel_id=1, source_target_pairs={{0,2},{1,3},{2,0},{3,1},{4,6},{5,7},{6,4},{7,5},{8,10},{9,11},{10,... | collective-permute-start | bytes 6291464 | tf_op jit(solution)/shard_map/ppermute | solution.py:90
  204.1 46.1 %copy-start.5 = (f32[2048]{0:T(1024)S(1)}, f32[2048]{0:T(1024)}, u32[]{:S(2)}) copy-start(f32[2048]{0:T(1024)} %param.17) | copy-start | bytes 24580
  263.9 281.7 %copy-start.1 = (bf16[512,2048]{1,0:T(8,128)(2,1)S(1)}, bf16[512,2048]{1,0:T(8,128)(2,1)}, u32[]{:S(2)}) copy-start(bf16[512,2048]{1,0:T(8,128)(2,1)} %param.15) | copy-start | bytes 6291460
  265.3 3.0 copy-start.8
  463.3 82.3 %copy-start.7 = (f32[128]{0:T(128)}, f32[128]{0:T(128)S(1)}, u32[]{:S(2)}) copy-start(f32[128]{0:T(128)S(1)} %get-tuple-element.7) | copy-start | bytes 1540
Sparse Core Ops, SparseCore 0:
  10.8 119.5 all-gather.1
  267.8 194.0 all-reduce.16
